TPU v7x, 32 devices: a whole 2x2x4 slice. The times are simulated.
32 devices in a mesh: dp: 4 (over x, core), expert: 8 (over z, y).
Axes of the slice: x: 2, y: 2, z: 4, core: 2. Of those that a mesh axis runs over, the one named last changes fastest.
Arguments:
- inputs: bfloat16 [512, 4096], P(('dp', 'expert')), may hold values from -6 to 6
- grad_out: bfloat16 [512, 4096], P(('dp', 'expert')), may hold values from -0.796875 to 0.796875
- labels: int32 [512, 1], P(('dp', 'expert')), may hold values from 0 to 7; in each aligned block of 16 rows (0 to 15, 16 to 31, ...) at most 3 rows name the same one
- w_gate: bfloat16 [4096, 57344], P('dp', 'expert'), may hold values from -0.09375 to 0.09375
- w_up: bfloat16 [4096, 57344], P('dp', 'expert'), may hold values from -0.09375 to 0.09375
- w_down: bfloat16 [57344, 4096], P('expert', 'dp'), may hold values from -0.0625 to 0.0625
Outputs:
- grad_in: bfloat16 [512, 4096], P(('dp', 'expert'))
- grad_gate: bfloat16 [4096, 57344], P('dp', 'expert')
- grad_up: bfloat16 [4096, 57344], P('dp', 'expert')
- grad_down: bfloat16 [57344, 4096], P('expert', 'dp')
Inputs may be any that keep to these rules, and one draw needn't show every extreme that they name: `labels`: among the 16 rows of one device no expert is named by more than 3 rows, a bound that some block reaches.
All inputs are finite; a program needn't handle non-finite values.
Results may differ from a plain program's by a relative error of at most 0.011.
Values may be sent and summed in bfloat16 or wider, within the bound.
No kernel may reach another device: no remote copies, remote signals or barrier semaphores. Data moves between devices by JAX's collectives and lax.ppermute only.
A program may use at most 192 MiB of HBM per device.

v0:
```python
import jax
import jax.numpy as jnp
from jax import lax
from jax.sharding import PartitionSpec as P

EXPERTS = 8


def nonlinear(gate, up, dhid):
    sig = jax.nn.sigmoid(gate)
    act = gate * sig
    hidden = (act * up).astype(jnp.bfloat16)
    d_up = (dhid * act).astype(jnp.bfloat16)
    d_gate = (dhid * up * sig * (1.0 + gate * (1.0 - sig))).astype(jnp.bfloat16)
    return (hidden, d_up, d_gate)


def contract_rows(left, right):
    return lax.dot_general(
        left, right, (((0,), (0,)), ((), ())), preferred_element_type=jnp.float32
    )


def on_device(inputs, grad_out, labels, w_gate, w_up, w_down):
    members = lax.axis_size("expert")
    replicas = lax.axis_size("dp")
    group = members // EXPERTS
    tok_count = inputs.shape[0]
    width = inputs.shape[1]
    capacity = 3 * tok_count // (2 * EXPERTS)
    label_col = labels[:, 0]
    onehot = (label_col[:, None] == jnp.arange(EXPERTS, dtype=jnp.int32)[None, :]).astype(jnp.int32)
    before = jnp.cumsum(onehot, axis=0) - onehot
    rank_in = jnp.sum(before * onehot, axis=1)
    slot_ids = label_col * capacity + rank_in

    def spread(values):
        buffer = jnp.zeros((EXPERTS * capacity, width), jnp.bfloat16).at[slot_ids].set(values)
        return jnp.repeat(buffer.reshape(EXPERTS, 1, capacity, width), group, axis=0)

    recv_in, recv_grad = (
        lax.all_to_all(
            lax.all_to_all(spread(inputs), "dp", split_axis=3, concat_axis=1, tiled=True),
            "expert",
            split_axis=0,
            concat_axis=0,
            tiled=True,
        ),
        lax.all_to_all(
            lax.all_to_all(spread(grad_out), "dp", split_axis=3, concat_axis=1, tiled=True),
            "expert",
            split_axis=0,
            concat_axis=0,
            tiled=True,
        ),
    )
    columns = width // replicas
    rows_in = recv_in.reshape(-1, columns)
    rows_grad = recv_grad.reshape(-1, columns)
    gate_part = jnp.dot(rows_in, w_gate, preferred_element_type=jnp.float32)
    up_part = jnp.dot(rows_in, w_up, preferred_element_type=jnp.float32)
    dhid_part = lax.dot_general(
        rows_grad, w_down, (((1,), (1,)), ((), ())), preferred_element_type=jnp.float32
    )
    gate, up, dhid = lax.psum((gate_part, up_part, dhid_part), "dp")
    hidden, d_up, d_gate = nonlinear(gate, up, dhid)
    d_rows = lax.dot_general(
        d_gate, w_gate, (((1,), (1,)), ((), ())), preferred_element_type=jnp.float32
    )
    d_rows = d_rows + lax.dot_general(
        d_up, w_up, (((1,), (1,)), ((), ())), preferred_element_type=jnp.float32
    )
    back_rows = lax.all_to_all(
        lax.all_to_all(
            d_rows.reshape(members, replicas, capacity, columns).astype(jnp.bfloat16),
            "dp",
            split_axis=1,
            concat_axis=3,
            tiled=True,
        ),
        "expert",
        split_axis=0,
        concat_axis=0,
        tiled=True,
    ).astype(jnp.float32)
    summed = jnp.sum(back_rows.reshape(EXPERTS, group, capacity, width), axis=1)
    grad_in = summed.reshape(EXPERTS * capacity, width)[slot_ids].astype(jnp.bfloat16)
    grad_gate = contract_rows(rows_in, d_gate).astype(jnp.bfloat16)
    grad_up = contract_rows(rows_in, d_up).astype(jnp.bfloat16)
    grad_down = contract_rows(hidden, rows_grad).astype(jnp.bfloat16)
    return (grad_in, grad_gate, grad_up, grad_down)


def solution(mesh):
    return jax.shard_map(
        on_device,
        mesh=mesh,
        in_specs=(
            P(("dp", "expert"), None),
            P(("dp", "expert"), None),
            P(("dp", "expert"), None),
            P("dp", "expert"),
            P("dp", "expert"),
            P("expert", "dp"),
        ),
        out_specs=(
            P(("dp", "expert"), None),
            P("dp", "expert"),
            P("dp", "expert"),
            P("expert", "dp"),
        ),
        check_vma=False,
    )
```

profile of v0, /device:TPU:0, one launch (start us, length us, event | category | flops | bytes accessed | tf_op | source)
XLA Modules:
  0.0 330.5 jit_solution(10850027350697886702)
XLA Ops:
  7.2 0.7 fusion.7
  7.9 0.8 select_reduce_fusion
  8.8 0.7 fusion.8
  9.4 1.2 scatter_custom_fusion.1
  10.8 4.6 %copy.38 = bf16[8,1,3,4096]{0,2,1,3:T(4,128)(2,1)} copy(bf16[8,1,3,4096]{3,2,0,1:T(4,128)(2,1)S(1)} %reshape_broadcast_in_dim_reshape.7) | data formatting | bytes 393216 | tf_op jit(solution)/shard_map/reshape;broadcast_in_dim;reshape | solution.py:39
  15.4 5.8 %reshape.60 = bf16[4,2,12288]{2,1,0:T(2,128)(2,1)} reshape(bf16[4096,1,3,8]{3,2,1,0:T(4,128)(2,1)} %bitcast.43) | data formatting | bytes 393216
  21.2 4.2 %all-to-all-start.2 = ((bf16[4,2,12288]{2,1,0:T(2,128)(2,1)}), bf16[4,2,12288]{2,1,0:T(2,128)(2,1)S(1)}, u32[]{:S(2)}, u32[]{:S(2)}) async-start(bf16[4,2,12288]{2,1,0:T(2,128)(2,1)} %reshape.60), calls=%async_computation.2 | async-start | bytes 393216 | tf_op jit(solution)/shard_map/all_to_all | solution.py:43
  25.4 1.2 scatter_custom_fusion
  26.8 4.6 %copy.34 = bf16[8,1,3,4096]{0,2,1,3:T(4,128)(2,1)} copy(bf16[8,1,3,4096]{3,2,0,1:T(4,128)(2,1)S(1)} %reshape_broadcast_in_dim_reshape.6) | data formatting | bytes 393216 | tf_op jit(solution)/shard_map/reshape;broadcast_in_dim;reshape | solution.py:39
  31.4 5.8 %reshape.62 = bf16[4,2,12288]{2,1,0:T(2,128)(2,1)} reshape(bf16[4096,1,3,8]{3,2,1,0:T(4,128)(2,1)} %bitcast.44) | data formatting | bytes 393216
  37.2 3.4 %all-to-all-start = ((bf16[4,2,12288]{2,1,0:T(2,128)(2,1)}), bf16[4,2,12288]{2,1,0:T(2,128)(2,1)S(1)}, u32[]{:S(2)}, u32[]{:S(2)}) async-start(bf16[4,2,12288]{2,1,0:T(2,128)(2,1)} %reshape.62), calls=%async_computation | async-start | bytes 393216 | tf_op jit(solution)/shard_map/all_to_all | solution.py:50
  40.6 4.8 %reshape.61 = bf16[4096,1,3,8]{3,2,1,0:T(4,128)(2,1)} reshape(bf16[4,2,12288]{2,1,0:T(2,128)(2,1)S(1)} %all-to-all-done.2) | data formatting | bytes 393216
  45.4 6.6 %copy.40 = bf16[8,4,3,1024]{3,1,2,0:T(4,128)(2,1)} copy(bf16[8,4,3,1024]{0,2,3,1:T(4,128)(2,1)} %bitcast.45) | data formatting | bytes 393216 | tf_op jit(solution)/shard_map/all_to_all | solution.py:43
  52.0 6.5 %all-to-all-start.3 = ((bf16[8,4,3,1024]{3,1,2,0:T(4,128)(2,1)}), bf16[8,4,3,1024]{3,1,2,0:T(4,128)(2,1)S(1)}, u32[]{:S(2)}, u32[]{:S(2)}) async-start(bf16[8,4,3,1024]{3,1,2,0:T(4,128)(2,1)} %copy.40), calls=%async_computation.3 | async-start | bytes 393216 | tf_op jit(solution)/shard_map/all_to_all | solution.py:42
  58.5 4.8 %reshape.63 = bf16[4096,1,3,8]{3,2,1,0:T(4,128)(2,1)} reshape(bf16[4,2,12288]{2,1,0:T(2,128)(2,1)S(1)} %all-to-all-done) | data formatting | bytes 393216
  63.2 6.7 %copy.36 = bf16[8,4,3,1024]{3,1,2,0:T(4,128)(2,1)} copy(bf16[8,4,3,1024]{0,2,3,1:T(4,128)(2,1)} %bitcast.46) | data formatting | bytes 393216 | tf_op jit(solution)/shard_map/all_to_all | solution.py:50
  69.9 6.0 %all-to-all-start.1 = ((bf16[8,4,3,1024]{3,1,2,0:T(4,128)(2,1)}), bf16[8,4,3,1024]{3,1,2,0:T(4,128)(2,1)S(1)}, u32[]{:S(2)}, u32[]{:S(2)}) async-start(bf16[8,4,3,1024]{3,1,2,0:T(4,128)(2,1)} %copy.36), calls=%async_computation.1 | async-start | bytes 393216 | tf_op jit(solution)/shard_map/all_to_all | solution.py:49
  76.4 9.2 %fusion.12 = f32[96,7168]{1,0:T(8,128)} fusion(bf16[96,1024]{1,0:T(8,128)(2,1)S(1)} %reshape.26, bf16[1024,7168]{1,0:T(8,128)(2,1)} %param.9), kind=kOutput, calls=%fused_computation.27 | convolution fusion | flops 1409286144 | bytes 17629184 | tf_op jit(solution)/shard_map/dot_general | solution.py:60
  85.6 9.2 %fusion.11 = f32[96,7168]{1,0:T(8,128)} fusion(bf16[96,1024]{1,0:T(8,128)(2,1)S(1)} %reshape.26, bf16[1024,7168]{1,0:T(8,128)(2,1)} %param.10), kind=kOutput, calls=%fused_computation.26 | convolution fusion | flops 1409286144 | bytes 17629184 | tf_op jit(solution)/shard_map/dot_general | solution.py:61
  95.0 11.3 %fusion.10 = f32[96,7168]{1,0:T(8,128)} fusion(bf16[96,1024]{1,0:T(8,128)(2,1)S(1)} %reshape.25, bf16[7168,1024]{1,0:T(8,128)(2,1)} %param.11), kind=kOutput, calls=%fused_computation.25 | convolution fusion | flops 1409286144 | bytes 17629184 | tf_op jit(solution)/shard_map/dot_general | solution.py:62
  106.4 153.3 %all-reduce.3.cloned.1.call-done = (f32[96,7168]{1,0:T(8,128)}, f32[96,7168]{1,0:T(8,128)}, f32[96,7168]{1,0:T(8,128)}) async-done(((f32[96,7168]{1,0:T(8,128)}, f32[96,7168]{1,0:T(8,128)}, f32[96,7168]{1,0:T(8,128)}), (f32[96,7168]{1,0:T(8,128)}, f32[96,7168]{1,0:T(8,128)}, f32[96,7168]{1,0:T(8,128)})) %all-reduce.3.cloned.1.call-update) | async-done | bytes 8257552 | tf_op jit(solution)/shard_map/psum | solution.py:65
  259.6 10.3 %convolution_convert_fusion = bf16[7168,1024]{1,0:T(8,128)(2,1)} fusion(bf16[96,1024]{1,0:T(8,128)(2,1)S(1)} %reshape.25, f32[96,7168]{1,0:T(8,128)} %get-tuple-element.6, f32[96,7168]{1,0:T(8,128)} %get-tuple-element.4), kind=kOutput, calls=%fused_computation.3 | convolution fusion | flops 1420754944 | bytes 20381696 | tf_op jit(solution)/shard_map/dot_general | solution.py:19
  270.0 4.0 %multiply_convert_fusion.1 = (bf16[96,7168]{1,0:T(8,128)(2,1)S(1)}, bf16[96,7168]{1,0:T(8,128)(2,1)S(1)}) fusion(f32[96,7168]{1,0:T(8,128)} %get-tuple-element.5, f32[96,7168]{1,0:T(8,128)S(1)} %copy-done, f32[96,7168]{1,0:T(8,128)} %get-tuple-element.6), kind=kLoop, calls=%fused_computation.7 | loop fusion | flops 8945664 | bytes 11010048 | tf_op jit(solution)/shard_map/convert_element_type | solution.py:13
  274.0 10.3 %fusion.13 = f32[96,1024]{1,0:T(8,128)S(1)} fusion(bf16[96,7168]{1,0:T(8,128)(2,1)S(1)} %get-tuple-element.8, bf16[1024,7168]{1,0:T(8,128)(2,1)} %param.9), kind=kOutput, calls=%fused_computation.28 | convolution fusion | flops 1409286144 | bytes 16449536 | tf_op jit(solution)/shard_map/dot_general | solution.py:67
  284.3 9.9 %fusion.1 = bf16[96,1024]{1,0:T(8,128)(2,1)S(1)} fusion(f32[96,1024]{1,0:T(8,128)S(1)} %fusion.13, bf16[96,7168]{1,0:T(8,128)(2,1)S(1)} %get-tuple-element.7, bf16[1024,7168]{1,0:T(8,128)(2,1)} %param.10), kind=kOutput, calls=%fused_computation.12 | convolution fusion | flops 1409482752 | bytes 16646144 | tf_op jit(solution)/shard_map/dot_general | solution.py:70
  294.3 0.8 copy.42
  295.1 3.6 %all-to-all-start.4 = ((bf16[8,4,3,1024]{3,0,2,1:T(8,128)(2,1)}), bf16[8,4,3,1024]{3,0,2,1:T(8,128)(2,1)S(1)}, u32[]{:S(2)}, u32[]{:S(2)}) async-start(bf16[8,4,3,1024]{3,0,2,1:T(8,128)(2,1)} %copy.42), calls=%async_computation.4 | async-start | bytes 393216 | tf_op jit(solution)/shard_map/all_to_all | solution.py:74
  298.8 7.6 %convolution_convert_fusion.1 = bf16[1024,7168]{1,0:T(8,128)(2,1)} fusion(bf16[96,1024]{1,0:T(8,128)(2,1)S(1)} %reshape.26, bf16[96,7168]{1,0:T(8,128)(2,1)S(1)} %get-tuple-element.7), kind=kOutput, calls=%fused_computation.4 | convolution fusion | flops 1416626176 | bytes 16252928 | tf_op jit(solution)/shard_map/dot_general | solution.py:19
  306.5 0.9 reshape.55
  307.4 5.5 %all-to-all-start.5 = ((bf16[8,1,3,4096]{3,2,1,0:T(4,128)(2,1)}), bf16[8,1,3,4096]{3,2,1,0:T(4,128)(2,1)S(1)}, u32[]{:S(2)}, u32[]{:S(2)}) async-start(bf16[8,1,3,4096]{3,2,1,0:T(4,128)(2,1)} %reshape.55), calls=%async_computation.5 | async-start | bytes 524288 | tf_op jit(solution)/shard_map/all_to_all | solution.py:73
  312.9 8.9 %convolution_convert_fusion.2 = bf16[1024,7168]{1,0:T(8,128)(2,1)} fusion(bf16[96,1024]{1,0:T(8,128)(2,1)S(1)} %reshape.26, bf16[96,7168]{1,0:T(8,128)(2,1)} %copy-done.1), kind=kOutput, calls=%fused_computation.5 | convolution fusion | flops 1416626176 | bytes 16252928 | tf_op jit(solution)/shard_map/dot_general | solution.py:19
  322.3 1.3 gather_fusion
  (23 shorter events, 2.0 us)
Async XLA Ops:
  21.2 16.0 %all-to-all-start.2 = ((bf16[4,2,12288]{2,1,0:T(2,128)(2,1)}), bf16[4,2,12288]{2,1,0:T(2,128)(2,1)S(1)}, u32[]{:S(2)}, u32[]{:S(2)}) async-start(bf16[4,2,12288]{2,1,0:T(2,128)(2,1)} %reshape.60), calls=%async_computation.2 | async-start | bytes 393216 | tf_op jit(solution)/shard_map/all_to_all | solution.py:43
  37.2 14.8 %all-to-all-start = ((bf16[4,2,12288]{2,1,0:T(2,128)(2,1)}), bf16[4,2,12288]{2,1,0:T(2,128)(2,1)S(1)}, u32[]{:S(2)}, u32[]{:S(2)}) async-start(bf16[4,2,12288]{2,1,0:T(2,128)(2,1)} %reshape.62), calls=%async_computation | async-start | bytes 393216 | tf_op jit(solution)/shard_map/all_to_all | solution.py:50
  52.0 17.9 %all-to-all-start.3 = ((bf16[8,4,3,1024]{3,1,2,0:T(4,128)(2,1)}), bf16[8,4,3,1024]{3,1,2,0:T(4,128)(2,1)S(1)}, u32[]{:S(2)}, u32[]{:S(2)}) async-start(bf16[8,4,3,1024]{3,1,2,0:T(4,128)(2,1)} %copy.40), calls=%async_computation.3 | async-start | bytes 393216 | tf_op jit(solution)/shard_map/all_to_all | solution.py:42
  69.9 24.8 %all-to-all-start.1 = ((bf16[8,4,3,1024]{3,1,2,0:T(4,128)(2,1)}), bf16[8,4,3,1024]{3,1,2,0:T(4,128)(2,1)S(1)}, u32[]{:S(2)}, u32[]{:S(2)}) async-start(bf16[8,4,3,1024]{3,1,2,0:T(4,128)(2,1)} %copy.36), calls=%async_computation.1 | async-start | bytes 393216 | tf_op jit(solution)/shard_map/all_to_all | solution.py:49
  75.9 183.8 %all-reduce.3.cloned.1.call-start = ((), (), s32[]{:S(2)}) async-start(), calls=%async_computation.6 | async-start | bytes 16515072 | tf_op jit(solution)/shard_map/psum | solution.py:65
  259.6 10.3 %copy-start = (f32[96,7168]{1,0:T(8,128)S(1)}, f32[96,7168]{1,0:T(8,128)}, u32[]{:S(2)}) copy-start(f32[96,7168]{1,0:T(8,128)} %get-tuple-element.4) | copy-start | bytes 8257540
  274.0 10.3 %copy-start.1 = (bf16[96,7168]{1,0:T(8,128)(2,1)}, bf16[96,7168]{1,0:T(8,128)(2,1)S(1)}, u32[]{:S(2)}) copy-start(bf16[96,7168]{1,0:T(8,128)(2,1)S(1)} %get-tuple-element.8) | copy-start | bytes 4128772
  295.1 11.2 %all-to-all-start.4 = ((bf16[8,4,3,1024]{3,0,2,1:T(8,128)(2,1)}), bf16[8,4,3,1024]{3,0,2,1:T(8,128)(2,1)S(1)}, u32[]{:S(2)}, u32[]{:S(2)}) async-start(bf16[8,4,3,1024]{3,0,2,1:T(8,128)(2,1)} %copy.42), calls=%async_computation.4 | async-start | bytes 393216 | tf_op jit(solution)/shard_map/all_to_all | solution.py:74
  307.4 14.8 %all-to-all-start.5 = ((bf16[8,1,3,4096]{3,2,1,0:T(4,128)(2,1)}), bf16[8,1,3,4096]{3,2,1,0:T(4,128)(2,1)S(1)}, u32[]{:S(2)}, u32[]{:S(2)}) async-start(bf16[8,1,3,4096]{3,2,1,0:T(4,128)(2,1)} %reshape.55), calls=%async_computation.5 | async-start | bytes 524288 | tf_op jit(solution)/shard_map/all_to_all | solution.py:73
Sparse Core Ops, SparseCore 0:
  106.5 153.1 all-reduce.2
where the time goes:
time: 332 us; the launch traced here: 330 us
  waiting for transfers between devices  154 us (46%)
  matrix products  76.6 us (23%)
  local copies, waits for them, and re-layouts  50.4 us (15%)
  starting transfers between devices  29.4 us (9%)
  between operations  14.2 us (4%)
  other arithmetic  6.24 us (2%)
    psum x1, waiting for transfers between devices, on_device(): gate, up, dhid = lax.psum((gate_part, up_part, dhid_part), 'dp')  153 us
    dot_general x3, matrix products, contract_rows(): lax.dot_general(left, right, (((0,), (0,)), ((), ())), preferred_element_...  26.9 us
    unnamed x8, local copies, waits for them, and re-layouts  21.2 us
    dot_general x1, matrix products, on_device(): lax.dot_general(rows_grad, w_down, (((1,), (1,)), ((), ())), preferred_el...  11.3 us
    dot_general x1, matrix products, on_device(): lax.dot_general(d_gate, w_gate, (((1,), (1,)), ((), ())), preferred_eleme...  10.3 us
    dot_general x1, matrix products, on_device(): lax.dot_general(d_up, w_up, (((1,), (1,)), ((), ())), preferred_element_t...  9.9 us
    another operation x4, local copies, waits for them, and re-layouts, spread(): jnp.repeat(buffer.reshape(EXPERTS, 1, capacity, width), group, axis=0)  9.43 us
    dot_general x1, matrix products, on_device(): gate_part = jnp.dot(rows_in, w_gate, preferred_element_type=jnp.float32)  9.16 us
  transfers between devices with their start and end apart: 7, of which 2 were waited for; matrix products, arithmetic and copies ran while one was open for 21% of the time, Pallas kernels for 0%

commit v1 on v0

--- a/solution.py
+++ b/solution.py
@@ -38,6 +38,25 @@
         buffer = jnp.zeros((EXPERTS * capacity, width), jnp.bfloat16).at[slot_ids].set(values)
         return jnp.repeat(buffer.reshape(EXPERTS, 1, capacity, width), group, axis=0)
 
+    def lead_state_in(inner_x):
+        across = "dp"
+        z1 = lax.axis_size(across)
+        top = lax.axis_index(across)
+        long_array, r2 = (z1, top)
+        heard = inner_x.shape[3] // long_array
+        f_next = list(inner_x.shape)
+        f_next[3] = heard
+        z_new = f_next[1]
+        f_next[1] = z_new * long_array
+        mat_out = jnp.zeros(f_next, inner_x.dtype)
+        for pp in range(long_array):
+            low = lax.dynamic_slice_in_dim(inner_x, (r2 ^ pp) * heard, heard, axis=3)
+            if pp:
+                e_next = list(map(lambda s: (s, s ^ pp), range(long_array)))
+                low = lax.ppermute(low, axis_name=across, perm=e_next)
+            mat_out = lax.dynamic_update_slice_in_dim(mat_out, low, (r2 ^ pp) * z_new, axis=1)
+        return mat_out
+
     recv_in, recv_grad = (
         lax.all_to_all(
             lax.all_to_all(spread(inputs), "dp", split_axis=3, concat_axis=1, tiled=True),
@@ -47,11 +66,7 @@
             tiled=True,
         ),
         lax.all_to_all(
-            lax.all_to_all(spread(grad_out), "dp", split_axis=3, concat_axis=1, tiled=True),
-            "expert",
-            split_axis=0,
-            concat_axis=0,
-            tiled=True,
+            lead_state_in(spread(grad_out)), "expert", split_axis=0, concat_axis=0, tiled=True
         ),
     )
     columns = width // replicas

time: 332 us -> 321 us (0.967)
  local copies, waits for them, and re-layouts: 50.4 us -> 40.7 us
    dynamic_update_slice x0 -> x4, local copies, waits for them, and re-layouts: none -> 10.9 us  [lead_state_in(): lax.dynamic_update_slice_in_dim(mat_out, low, (r2 ^ pp) * z_new, axis=1)]
    unnamed x8 -> x6, local copies, waits for them, and re-layouts: 21.2 us -> 10.6 us
    all_to_all x2 -> x1, local copies, waits for them, and re-layouts: 6.79 us -> 0.14 us  [on_device(): lax.all_to_all(lead_state_in(spread(grad_out)), 'expert', split_axis=0, c...]
    another operation x4 -> x3, local copies, waits for them, and re-layouts: 9.43 us -> 4.84 us  [spread(): jnp.repeat(buffer.reshape(EXPERTS, 1, capacity, width), group, axis=0)]
    all_to_all x2 -> x1, starting transfers between devices: 9.35 us -> 6.34 us  [on_device(): lax.all_to_all(lead_state_in(spread(grad_out)), 'expert', split_axis=0, c...]
  transfers between devices with their start and end apart: 7 -> 9, of which waited for: 2 -> 2; matrix products, arithmetic and copies ran while one was open for 21% -> 17% of each run, Pallas kernels for 0% -> 0%
where the time goes in v1:
time: 321 us; the launch traced here: 319 us
  waiting for transfers between devices  153 us (48%)
  matrix products  76.6 us (24%)
  local copies, waits for them, and re-layouts  40.7 us (13%)
  starting transfers between devices  28.2 us (9%)
  between operations  14.2 us (4%)
  other arithmetic  6.24 us (2%)
    psum x1, waiting for transfers between devices, on_device(): gate, up, dhid = lax.psum((gate_part, up_part, dhid_part), 'dp')  153 us
    dot_general x3, matrix products, contract_rows(): lax.dot_general(left, right, (((0,), (0,)), ((), ())), preferred_element_...  26.9 us
    dot_general x1, matrix products, on_device(): lax.dot_general(rows_grad, w_down, (((1,), (1,)), ((), ())), preferred_el...  11.3 us
    dynamic_update_slice x4, local copies, waits for them, and re-layouts, lead_state_in(): lax.dynamic_update_slice_in_dim(mat_out, low, (r2 ^ pp) * z_new, axis=1)  10.9 us
    unnamed x6, local copies, waits for them, and re-layouts  10.6 us
    dot_general x1, matrix products, on_device(): lax.dot_general(d_gate, w_gate, (((1,), (1,)), ((), ())), preferred_eleme...  10.3 us
    dot_general x1, matrix products, on_device(): lax.dot_general(d_up, w_up, (((1,), (1,)), ((), ())), preferred_element_t...  9.9 us
    dot_general x1, matrix products, on_device(): gate_part = jnp.dot(rows_in, w_gate, preferred_element_type=jnp.float32)  9.16 us
  transfers between devices with their start and end apart: 9, of which 2 were waited for; matrix products, arithmetic and copies ran while one was open for 17% of the time, Pallas kernels for 0%

profile of v1, /device:TPU:0, one launch (start us, length us, event | category | flops | bytes accessed | tf_op | source)
XLA Modules:
  0.0 319.3 jit_solution(5754761123755076392)
XLA Ops:
  7.2 0.7 fusion.7
  7.9 0.8 select_reduce_fusion
  9.4 1.2 scatter_custom_fusion.1
  10.8 4.6 %copy.43 = bf16[8,1,3,4096]{0,2,1,3:T(4,128)(2,1)} copy(bf16[8,1,3,4096]{3,2,0,1:T(4,128)(2,1)S(1)} %reshape_broadcast_in_dim_reshape.7) | data formatting | bytes 393216 | tf_op jit(solution)/shard_map/reshape;broadcast_in_dim;reshape | solution.py:39
  15.4 5.8 %reshape.60 = bf16[4,2,12288]{2,1,0:T(2,128)(2,1)} reshape(bf16[4096,1,3,8]{3,2,1,0:T(4,128)(2,1)} %bitcast.36) | data formatting | bytes 393216
  21.2 4.2 %all-to-all-start.1 = ((bf16[4,2,12288]{2,1,0:T(2,128)(2,1)}), bf16[4,2,12288]{2,1,0:T(2,128)(2,1)S(1)}, u32[]{:S(2)}, u32[]{:S(2)}) async-start(bf16[4,2,12288]{2,1,0:T(2,128)(2,1)} %reshape.60), calls=%async_computation.1 | async-start | bytes 393216 | tf_op jit(solution)/shard_map/all_to_all | solution.py:62
  25.4 1.2 scatter_custom_fusion
  27.5 1.7 collective-permute-start.1
  29.3 0.7 broadcast_in_dim.2
  30.1 2.7 dynamic_update_slice.12
  32.9 2.7 dynamic_update_slice.13
  35.7 2.7 dynamic_update_slice.14
  38.5 2.7 dynamic_update_slice.15
  41.3 6.3 %all-to-all-start = ((bf16[8,4,3,1024]{3,1,2,0:T(4,128)(2,1)}), bf16[8,4,3,1024]{3,1,2,0:T(4,128)(2,1)S(1)}, u32[]{:S(2)}, u32[]{:S(2)}) async-start(bf16[8,4,3,1024]{3,1,2,0:T(4,128)(2,1)} %dynamic_update_slice.15), calls=%async_computation | async-start | bytes 393216 | tf_op jit(solution)/shard_map/all_to_all | solution.py:68
  47.6 4.8 %reshape.61 = bf16[4096,1,3,8]{3,2,1,0:T(4,128)(2,1)} reshape(bf16[4,2,12288]{2,1,0:T(2,128)(2,1)S(1)} %all-to-all-done.1) | data formatting | bytes 393216
  52.4 6.6 %copy.45 = bf16[8,4,3,1024]{3,1,2,0:T(4,128)(2,1)} copy(bf16[8,4,3,1024]{0,2,3,1:T(4,128)(2,1)} %bitcast.37) | data formatting | bytes 393216 | tf_op jit(solution)/shard_map/all_to_all | solution.py:62
  59.0 6.0 %all-to-all-start.2 = ((bf16[8,4,3,1024]{3,1,2,0:T(4,128)(2,1)}), bf16[8,4,3,1024]{3,1,2,0:T(4,128)(2,1)S(1)}, u32[]{:S(2)}, u32[]{:S(2)}) async-start(bf16[8,4,3,1024]{3,1,2,0:T(4,128)(2,1)} %copy.45), calls=%async_computation.2 | async-start | bytes 393216 | tf_op jit(solution)/shard_map/all_to_all | solution.py:61
  65.6 11.3 %fusion.10 = f32[96,7168]{1,0:T(8,128)} fusion(bf16[96,1024]{1,0:T(8,128)(2,1)S(1)} %reshape.25, bf16[7168,1024]{1,0:T(8,128)(2,1)} %param.11), kind=kOutput, calls=%fused_computation.29 | convolution fusion | flops 1409286144 | bytes 17629184 | tf_op jit(solution)/shard_map/dot_general | solution.py:77
  77.2 9.2 %fusion.12 = f32[96,7168]{1,0:T(8,128)} fusion(bf16[96,1024]{1,0:T(8,128)(2,1)S(1)} %reshape.26, bf16[1024,7168]{1,0:T(8,128)(2,1)} %param.9), kind=kOutput, calls=%fused_computation.31 | convolution fusion | flops 1409286144 | bytes 17629184 | tf_op jit(solution)/shard_map/dot_general | solution.py:75
  86.3 9.2 %fusion.11 = f32[96,7168]{1,0:T(8,128)} fusion(bf16[96,1024]{1,0:T(8,128)(2,1)S(1)} %reshape.26, bf16[1024,7168]{1,0:T(8,128)(2,1)} %param.10), kind=kOutput, calls=%fused_computation.30 | convolution fusion | flops 1409286144 | bytes 17629184 | tf_op jit(solution)/shard_map/dot_general | solution.py:76
  95.5 153.0 %all-reduce.3.cloned.1.call-done = (f32[96,7168]{1,0:T(8,128)}, f32[96,7168]{1,0:T(8,128)}, f32[96,7168]{1,0:T(8,128)}) async-done(((f32[96,7168]{1,0:T(8,128)}, f32[96,7168]{1,0:T(8,128)}, f32[96,7168]{1,0:T(8,128)}), (f32[96,7168]{1,0:T(8,128)}, f32[96,7168]{1,0:T(8,128)}, f32[96,7168]{1,0:T(8,128)})) %all-reduce.3.cloned.1.call-update) | async-done | bytes 8257552 | tf_op jit(solution)/shard_map/psum | solution.py:80
  248.5 10.3 %convolution_convert_fusion = bf16[7168,1024]{1,0:T(8,128)(2,1)} fusion(bf16[96,1024]{1,0:T(8,128)(2,1)S(1)} %reshape.25, f32[96,7168]{1,0:T(8,128)} %get-tuple-element.6, f32[96,7168]{1,0:T(8,128)} %get-tuple-element.4), kind=kOutput, calls=%fused_computation.3 | convolution fusion | flops 1420754944 | bytes 20381696 | tf_op jit(solution)/shard_map/dot_general | solution.py:19
  258.9 4.0 %multiply_convert_fusion.1 = (bf16[96,7168]{1,0:T(8,128)(2,1)S(1)}, bf16[96,7168]{1,0:T(8,128)(2,1)S(1)}) fusion(f32[96,7168]{1,0:T(8,128)} %get-tuple-element.5, f32[96,7168]{1,0:T(8,128)S(1)} %copy-done, f32[96,7168]{1,0:T(8,128)} %get-tuple-element.6), kind=kLoop, calls=%fused_computation.7 | loop fusion | flops 8945664 | bytes 11010048 | tf_op jit(solution)/shard_map/convert_element_type | solution.py:13
  262.8 10.3 %fusion.13 = f32[96,1024]{1,0:T(8,128)S(1)} fusion(bf16[96,7168]{1,0:T(8,128)(2,1)S(1)} %get-tuple-element.8, bf16[1024,7168]{1,0:T(8,128)(2,1)} %param.9), kind=kOutput, calls=%fused_computation.32 | convolution fusion | flops 1409286144 | bytes 16449536 | tf_op jit(solution)/shard_map/dot_general | solution.py:82
  273.1 9.9 %fusion.1 = bf16[96,1024]{1,0:T(8,128)(2,1)S(1)} fusion(f32[96,1024]{1,0:T(8,128)S(1)} %fusion.13, bf16[96,7168]{1,0:T(8,128)(2,1)S(1)} %get-tuple-element.7, bf16[1024,7168]{1,0:T(8,128)(2,1)} %param.10), kind=kOutput, calls=%fused_computation.12 | convolution fusion | flops 1409482752 | bytes 16646144 | tf_op jit(solution)/shard_map/dot_general | solution.py:85
  283.2 0.8 copy.47
  284.0 3.6 %all-to-all-start.3 = ((bf16[8,4,3,1024]{3,0,2,1:T(8,128)(2,1)}), bf16[8,4,3,1024]{3,0,2,1:T(8,128)(2,1)S(1)}, u32[]{:S(2)}, u32[]{:S(2)}) async-start(bf16[8,4,3,1024]{3,0,2,1:T(8,128)(2,1)} %copy.47), calls=%async_computation.3 | async-start | bytes 393216 | tf_op jit(solution)/shard_map/all_to_all | solution.py:89
  287.6 7.6 %convolution_convert_fusion.1 = bf16[1024,7168]{1,0:T(8,128)(2,1)} fusion(bf16[96,1024]{1,0:T(8,128)(2,1)S(1)} %reshape.26, bf16[96,7168]{1,0:T(8,128)(2,1)S(1)} %get-tuple-element.7), kind=kOutput, calls=%fused_computation.4 | convolution fusion | flops 1416626176 | bytes 16252928 | tf_op jit(solution)/shard_map/dot_general | solution.py:19
  295.4 0.9 reshape.55
  296.2 5.5 %all-to-all-start.4 = ((bf16[8,1,3,4096]{3,2,1,0:T(4,128)(2,1)}), bf16[8,1,3,4096]{3,2,1,0:T(4,128)(2,1)S(1)}, u32[]{:S(2)}, u32[]{:S(2)}) async-start(bf16[8,1,3,4096]{3,2,1,0:T(4,128)(2,1)} %reshape.55), calls=%async_computation.4 | async-start | bytes 524288 | tf_op jit(solution)/shard_map/all_to_all | solution.py:88
  301.8 8.9 %convolution_convert_fusion.2 = bf16[1024,7168]{1,0:T(8,128)(2,1)} fusion(bf16[96,1024]{1,0:T(8,128)(2,1)S(1)} %reshape.26, bf16[96,7168]{1,0:T(8,128)(2,1)} %copy-done.1), kind=kOutput, calls=%fused_computation.5 | convolution fusion | flops 1416626176 | bytes 16252928 | tf_op jit(solution)/shard_map/dot_general | solution.py:19
  311.2 1.3 gather_fusion
  (33 shorter events, 3.7 us)
Async XLA Ops:
  21.2 20.1 %all-to-all-start.1 = ((bf16[4,2,12288]{2,1,0:T(2,128)(2,1)}), bf16[4,2,12288]{2,1,0:T(2,128)(2,1)S(1)}, u32[]{:S(2)}, u32[]{:S(2)}) async-start(bf16[4,2,12288]{2,1,0:T(2,128)(2,1)} %reshape.60), calls=%async_computation.1 | async-start | bytes 393216 | tf_op jit(solution)/shard_map/all_to_all | solution.py:62
  26.9 5.9 %collective-permute-start = (bf16[8,1,3,1024]{3,2,0,1:T(4,128)(2,1)S(1)}, bf16[8,1,3,1024]{3,2,0,1:T(4,128)(2,1)S(1)}, u32[]{:S(2)}, u32[]{:S(2)}) collective-permute-start(bf16[8,1,3,1024]{3,2,0,1:T(4,128)(2,1)S(1)} %get-tuple-element.11), channel_id=1, source_target_pairs={{0,8},{8,0},{16,24},{24,16},{1,9},{9,1},{17,25},{25,17},{2,10},{10... | collective-permute-start | bytes 147464 | tf_op jit(solution)/shard_map/ppermute | solution.py:56
  27.5 8.1 %collective-permute-start.1 = (bf16[8,1,3,1024]{3,2,0,1:T(4,128)(2,1)S(1)}, bf16[8,1,3,1024]{3,2,0,1:T(4,128)(2,1)S(1)}, u32[]{:S(2)}, u32[]{:S(2)}) collective-permute-start(bf16[8,1,3,1024]{3,2,0,1:T(4,128)(2,1)S(1)} %get-tuple-element.10), channel_id=1, source_target_pairs={{0,16},{8,24},{16,0},{24,8},{1,17},{9,25},{17,1},{25,9},{2,18},{10... | collective-permute-start | bytes 147464 | tf_op jit(solution)/shard_map/ppermute | solution.py:56
  29.2 9.3 %collective-permute-start.2 = (bf16[8,1,3,1024]{3,2,0,1:T(4,128)(2,1)S(1)}, bf16[8,1,3,1024]{3,2,0,1:T(4,128)(2,1)S(1)}, u32[]{:S(2)}, u32[]{:S(2)}) collective-permute-start(bf16[8,1,3,1024]{3,2,0,1:T(4,128)(2,1)S(1)} %get-tuple-element.9), channel_id=1, source_target_pairs={{0,24},{8,16},{16,8},{24,0},{1,25},{9,17},{17,9},{25,1},{2,26},{10... | collective-permute-start | bytes 147464 | tf_op jit(solution)/shard_map/ppermute | solution.py:56
  41.3 17.8 %all-to-all-start = ((bf16[8,4,3,1024]{3,1,2,0:T(4,128)(2,1)}), bf16[8,4,3,1024]{3,1,2,0:T(4,128)(2,1)S(1)}, u32[]{:S(2)}, u32[]{:S(2)}) async-start(bf16[8,4,3,1024]{3,1,2,0:T(4,128)(2,1)} %dynamic_update_slice.15), calls=%async_computation | async-start | bytes 393216 | tf_op jit(solution)/shard_map/all_to_all | solution.py:68
  59.0 17.8 %all-to-all-start.2 = ((bf16[8,4,3,1024]{3,1,2,0:T(4,128)(2,1)}), bf16[8,4,3,1024]{3,1,2,0:T(4,128)(2,1)S(1)}, u32[]{:S(2)}, u32[]{:S(2)}) async-start(bf16[8,4,3,1024]{3,1,2,0:T(4,128)(2,1)} %copy.45), calls=%async_computation.2 | async-start | bytes 393216 | tf_op jit(solution)/shard_map/all_to_all | solution.py:61
  65.0 183.5 %all-reduce.3.cloned.1.call-start = ((), (), s32[]{:S(2)}) async-start(), calls=%async_computation.5 | async-start | bytes 16515072 | tf_op jit(solution)/shard_map/psum | solution.py:80
  248.5 10.4 %copy-start = (f32[96,7168]{1,0:T(8,128)S(1)}, f32[96,7168]{1,0:T(8,128)}, u32[]{:S(2)}) copy-start(f32[96,7168]{1,0:T(8,128)} %get-tuple-element.4) | copy-start | bytes 8257540
  262.8 10.3 %copy-start.1 = (bf16[96,7168]{1,0:T(8,128)(2,1)}, bf16[96,7168]{1,0:T(8,128)(2,1)S(1)}, u32[]{:S(2)}) copy-start(bf16[96,7168]{1,0:T(8,128)(2,1)S(1)} %get-tuple-element.8) | copy-start | bytes 4128772
  284.0 11.2 %all-to-all-start.3 = ((bf16[8,4,3,1024]{3,0,2,1:T(8,128)(2,1)}), bf16[8,4,3,1024]{3,0,2,1:T(8,128)(2,1)S(1)}, u32[]{:S(2)}, u32[]{:S(2)}) async-start(bf16[8,4,3,1024]{3,0,2,1:T(8,128)(2,1)} %copy.47), calls=%async_computation.3 | async-start | bytes 393216 | tf_op jit(solution)/shard_map/all_to_all | solution.py:89
  296.2 14.8 %all-to-all-start.4 = ((bf16[8,1,3,4096]{3,2,1,0:T(4,128)(2,1)}), bf16[8,1,3,4096]{3,2,1,0:T(4,128)(2,1)S(1)}, u32[]{:S(2)}, u32[]{:S(2)}) async-start(bf16[8,1,3,4096]{3,2,1,0:T(4,128)(2,1)} %reshape.55), calls=%async_computation.4 | async-start | bytes 524288 | tf_op jit(solution)/shard_map/all_to_all | solution.py:88
Sparse Core Ops, SparseCore 0:
  95.6 152.8 all-reduce.2
